TPU v7x, 256 devices: a whole 4x4x8 slice. The times are simulated.
256 devices in a mesh: batch: 16 (over x_hi, z), dom: 16 (over x_lo, y, core).
Axes of the slice: x: 4 (x_hi: 2, x_lo: 2; x = x_hi * 2 + x_lo), y: 4, z: 8, core: 2. Of those that a mesh axis runs over, the one named last changes fastest.
Arguments:
- inputs: bfloat16 [32, 64, 68, 256], P('batch', 'dom'), may hold values from -70 to 70
- saved_q: bfloat16 [32, 64, 68, 256], P('batch', 'dom'), may hold values from -6.5 to 6.5
- saved_k: bfloat16 [32, 64, 68, 256], P('batch', 'dom'), may hold values from -6.5 to 6.5
- saved_v: bfloat16 [32, 64, 68, 256], P('batch', 'dom'), may hold values from -6 to 6
- attended: bfloat16 [32, 64, 68, 256], P('batch', 'dom'), may hold values from -6 to 6
- out_cot: bfloat16 [32, 64, 68, 256], P('batch', 'dom'), may hold values from -6 to 6
- conv_weight: bfloat16 [9, 256, 256], replicated, may hold values from -0.125 to 0.125
- qkv_weight: bfloat16 [256, 768], replicated, may hold values from -0.375 to 0.375
- out_weight: bfloat16 [256, 256], replicated, may hold values from -0.375 to 0.375
- norm_gain: float32 [256], replicated, may hold values from 0.5 to 1.5
- norm_shift: float32 [256], replicated, may hold values from -2.5 to 2.5
Outputs:
- input_grad: bfloat16 [32, 64, 68, 256], P('batch', 'dom')
- conv_grad: float32 [9, 256, 256], replicated
- qkv_grad: float32 [256, 768], replicated
- out_grad: float32 [256, 256], replicated
- gain_grad: float32 [256], replicated
- shift_grad: float32 [256], replicated
All inputs are finite; a program needn't handle non-finite values.
Results may differ from a plain program's by a relative error of at most 0.011.
Values may be sent and summed in bfloat16 or wider, within the bound.
No kernel may reach another device: no remote copies, remote signals or barrier semaphores. Data moves between devices by JAX's collectives and lax.ppermute only.
A program may use at most 128 MiB of HBM per device.

v0:
```python
import jax
import jax.numpy as jnp
from jax import lax
from jax.sharding import PartitionSpec as P

HEADS = 1
GROUPS = 32
EPSILON = 1e-05


def with_halo(cells, sides, width):
    for axis, dim in sides:
        count = lax.axis_size(axis)
        ends = count - 1
        head = lax.slice_in_dim(cells, 0, width, axis=dim)
        tail = lax.slice_in_dim(cells, cells.shape[dim] - width, cells.shape[dim], axis=dim)
        cells = jnp.concatenate(
            [
                lax.ppermute(tail, axis, [(i, (i + 1) % count) for i in range(ends)]),
                cells,
                lax.ppermute(head, axis, [((i + 1) % count, i) for i in range(ends)]),
            ],
            axis=dim,
        )
    return cells


def dom_psum(values):
    count = lax.axis_size("dom")
    step = 1
    while step < count:
        values = values + lax.ppermute(values, "dom", [(i, i ^ step) for i in range(count)])
        step *= 2
    return values


def dom_gather(values):
    count = lax.axis_size("dom")
    me = lax.axis_index("dom")
    values = values[None]
    step = 1
    while step < count:
        got = lax.ppermute(values, "dom", [(i, i ^ step) for i in range(count)])
        upper = me // step % 2 == 1
        values = jnp.where(upper, jnp.concatenate([got, values]), jnp.concatenate([values, got]))
        step *= 2
    return values


MESH_AXES = ("batch", "dom")
CORE0_BITS = (1, 3, 4, 2, 7, 5, 6)
CORE1_BITS = (4, 1, 3, 5, 2, 7, 6)


def mesh_psum(values):
    sizes = (lax.axis_size("batch"), lax.axis_size("dom"))
    if sizes != (16, 16):
        return lax.psum(values, MESH_AXES)
    count = 256
    me = lax.axis_index(MESH_AXES)
    core = me % 2
    steps = [(0, 0)] + list(zip(CORE0_BITS, CORE1_BITS))
    chosen = []
    for bit0, bit1 in steps:
        half = values.shape[0] // 2
        upper = jnp.where(core == 0, me >> bit0 & 1, me >> bit1 & 1) == 1
        low, high = (values[:half], values[half:])
        send = jnp.where(upper, low, high)
        keep = jnp.where(upper, high, low)
        pairs = [(i, i ^ 1 << (bit0 if i % 2 == 0 else bit1)) for i in range(count)]
        values = keep + lax.ppermute(send, MESH_AXES, pairs)
        chosen.append((upper, pairs))
    for upper, pairs in reversed(chosen):
        got = lax.ppermute(values, MESH_AXES, pairs)
        values = jnp.where(upper, jnp.concatenate([got, values]), jnp.concatenate([values, got]))
    return values


def per_channel(values, group_width):
    return jnp.repeat(values, group_width, axis=-1)[:, None, None, :]


def body(
    inputs,
    saved_q,
    saved_k,
    saved_v,
    attended,
    out_cot,
    conv_weight,
    qkv_weight,
    out_weight,
    norm_gain,
    norm_shift,
):
    samples, row_count, col_count, chan_count = inputs.shape
    tok_count = row_count * col_count
    group_width = chan_count // GROUPS
    head_width = chan_count // HEADS
    score_scale = head_width ** (-0.5)
    count = row_count * col_count * group_width * lax.axis_size("dom")
    f32 = jnp.float32
    bf16 = jnp.bfloat16
    input_wide = inputs.astype(f32)
    grouped = input_wide.reshape(samples, row_count, col_count, GROUPS, group_width)
    group_sums = dom_psum(jnp.stack([grouped.sum((1, 2, 4)), (grouped * grouped).sum((1, 2, 4))]))
    group_mean = group_sums[0] / count
    group_var = group_sums[1] / count - group_mean * group_mean
    inv_std = lax.rsqrt(group_var + EPSILON)
    normed = (input_wide - per_channel(group_mean, group_width)) * per_channel(inv_std, group_width)
    pre_act = normed * norm_gain + norm_shift
    sigmoid_pre = jax.nn.sigmoid(pre_act)
    activated = (pre_act * sigmoid_pre).astype(bf16)
    padded = with_halo(activated, (("dom", 1),), 1)
    padded = jnp.pad(padded, ((0, 0), (0, 0), (1, 1), (0, 0)))

    def shifted(source, row_start, col_start):
        return source[
            :, row_start : row_start + row_count, col_start : col_start + col_count, :
        ].reshape(-1, chan_count)

    conv_sum = input_wide.reshape(-1, chan_count)
    for tap_index in range(9):
        row_off = tap_index // 3 - 1
        col_off = tap_index % 3 - 1
        conv_sum = conv_sum + jnp.dot(
            shifted(padded, 1 + row_off, 1 + col_off),
            conv_weight[tap_index],
            preferred_element_type=f32,
        )
    residual = conv_sum.astype(bf16)
    out_flat = out_cot.reshape(-1, chan_count)
    attended_flat = attended.reshape(-1, chan_count)
    out_grad = jnp.einsum("nc,nd->cd", attended_flat, out_flat, preferred_element_type=f32)
    d_attended = jnp.einsum("nd,cd->nc", out_flat, out_weight, preferred_element_type=f32).astype(
        bf16
    )

    def split_heads(values):
        return values.reshape(samples, -1, HEADS, head_width)

    def scores(left, right):
        return jnp.einsum("sqhd,skhd->shqk", left, right, preferred_element_type=f32) * score_scale

    q_rows = saved_q.reshape(samples, tok_count, chan_count)
    k_rows = saved_k.reshape(samples, tok_count, chan_count)
    v_rows = saved_v.reshape(samples, tok_count, chan_count)
    do_rows = d_attended.reshape(samples, tok_count, chan_count)
    q_heads = split_heads(q_rows)
    k_heads = split_heads(k_rows)
    v_heads = split_heads(v_rows)
    do_heads = split_heads(do_rows)
    row_dot = jnp.einsum(
        "sqhd,sqhd->sqh",
        split_heads(attended.reshape(samples, tok_count, chan_count)),
        do_heads,
        preferred_element_type=f32,
    )
    row_dot_t = row_dot.transpose(0, 2, 1)

    def grad_terms(query_heads, dout_heads, key_heads, value_heads, log_norm_t, dot_t):
        softmax_p = jnp.exp(scores(query_heads, key_heads) - log_norm_t[..., None])
        d_probs = jnp.einsum("sqhd,skhd->shqk", dout_heads, value_heads, preferred_element_type=f32)
        d_scores = (softmax_p * (d_probs - dot_t[..., None])).astype(bf16)
        return (softmax_p.astype(bf16), d_scores)

    row_max = jnp.full((samples, HEADS, tok_count), -jnp.inf, f32)
    row_total = jnp.zeros((samples, HEADS, tok_count), f32)
    logits = scores(q_heads, split_heads(lax.all_gather(k_rows, "dom", axis=1, tiled=True)))
    new_max = logits.max(-1)
    row_total = row_total * jnp.exp(row_max - new_max) + jnp.exp(logits - new_max[..., None]).sum(
        -1
    )
    row_max, row_total = (new_max, row_total)
    log_norm = row_max + jnp.log(row_total)
    shard_piece = (
        lax.all_gather(k_rows, "dom", axis=1, tiled=True),
        lax.all_gather(v_rows, "dom", axis=1, tiled=True),
    )
    key_heads = split_heads(shard_piece[0])
    value_heads = split_heads(shard_piece[1])
    p_half, d_scores = grad_terms(q_heads, do_heads, key_heads, value_heads, log_norm, row_dot_t)
    q_accum = jnp.einsum("shqk,skhd->sqhd", d_scores, key_heads, preferred_element_type=f32)
    stats_local = dom_gather(jnp.stack([log_norm.transpose(0, 2, 1), row_dot]))
    stats_all = stats_local.transpose(1, 2, 0, 3, 4).reshape(2, samples, -1, HEADS)
    shard_piece = (
        lax.all_gather(q_rows, "dom", axis=1, tiled=True),
        lax.all_gather(do_rows, "dom", axis=1, tiled=True),
    )
    query_heads = split_heads(shard_piece[0])
    dout_heads = split_heads(shard_piece[1])
    norm_piece = stats_all[0].transpose(0, 2, 1)
    dot_piece = stats_all[1].transpose(0, 2, 1)
    p_half, d_scores = grad_terms(query_heads, dout_heads, k_heads, v_heads, norm_piece, dot_piece)
    k_accum = jnp.einsum("shqk,sqhd->skhd", d_scores, query_heads, preferred_element_type=f32)
    v_accum = jnp.einsum("shqk,sqhd->skhd", p_half, dout_heads, preferred_element_type=f32)
    k_accum, v_accum = (k_accum, v_accum)
    k_grad = (k_accum * score_scale).astype(bf16).reshape(samples, tok_count, chan_count)
    v_grad = v_accum.astype(bf16).reshape(samples, tok_count, chan_count)
    q_grad = (q_accum * score_scale).astype(bf16).reshape(samples, tok_count, chan_count)
    proj_grad = jnp.concatenate([q_grad, k_grad, v_grad], axis=-1).reshape(-1, 3 * chan_count)
    qkv_local = jnp.einsum("nc,nd->cd", residual, proj_grad, preferred_element_type=f32)
    d_residual = (
        out_flat.astype(f32)
        + jnp.einsum("nd,cd->nc", proj_grad, qkv_weight, preferred_element_type=f32)
    ).astype(bf16)
    d_res_map = d_residual.reshape(samples, row_count, col_count, chan_count)
    d_padded = with_halo(d_res_map, (("dom", 1),), 1)
    d_padded = jnp.pad(d_padded, ((0, 0), (0, 0), (1, 1), (0, 0)))
    conv_parts = []
    d_act = jnp.zeros((samples * tok_count, chan_count), f32)
    for tap_index in range(9):
        row_off = tap_index // 3 - 1
        col_off = tap_index % 3 - 1
        conv_parts.append(
            jnp.einsum(
                "nc,nd->cd",
                shifted(padded, 1 + row_off, 1 + col_off),
                d_residual,
                preferred_element_type=f32,
            )
        )
        d_act = d_act + jnp.einsum(
            "nd,cd->nc",
            shifted(d_padded, 1 - row_off, 1 - col_off),
            conv_weight[tap_index],
            preferred_element_type=f32,
        )
    conv_local = jnp.stack(conv_parts)
    d_pre = (
        d_act.reshape(samples, row_count, col_count, chan_count)
        * sigmoid_pre
        * (1.0 + pre_act * (1.0 - sigmoid_pre))
    )
    gain_local = (d_pre * normed).sum((0, 1, 2))
    shift_local = d_pre.sum((0, 1, 2))
    scaled = d_pre * norm_gain
    scaled_groups = scaled.reshape(samples, row_count, col_count, GROUPS, group_width)
    product_groups = (scaled * normed).reshape(samples, row_count, col_count, GROUPS, group_width)
    back_sums = dom_psum(jnp.stack([scaled_groups.sum((1, 2, 4)), product_groups.sum((1, 2, 4))]))
    first = back_sums[0] / count
    second = back_sums[1] / count
    input_grad = (
        d_res_map.astype(f32)
        + per_channel(inv_std, group_width)
        * (scaled - per_channel(first, group_width) - normed * per_channel(second, group_width))
    ).astype(bf16)
    parts = (out_grad, qkv_local, conv_local, gain_local, shift_local)
    flat = jnp.concatenate([part.reshape(-1) for part in parts])
    total = flat.shape[0]
    padded_len = -(-total // 32768) * 32768
    flat = mesh_psum(jnp.pad(flat, (0, padded_len - total)))
    pieces = []
    offset = 0
    for part in parts:
        pieces.append(flat[offset : offset + part.size].reshape(part.shape))
        offset += part.size
    out_grad, qkv_grad, conv_grad, gain_grad, shift_grad = pieces
    return (input_grad, conv_grad, qkv_grad, out_grad, gain_grad, shift_grad)


def solution(mesh):
    placed = (
        P("batch", "dom", None, None),
        P("batch", "dom", None, None),
        P("batch", "dom", None, None),
        P("batch", "dom", None, None),
        P("batch", "dom", None, None),
        P("batch", "dom", None, None),
        P(),
        P(),
        P(),
        P(),
        P(),
    )
    return jax.shard_map(
        body,
        mesh=mesh,
        in_specs=placed,
        out_specs=(P("batch", "dom", None, None), P(), P(), P(), P(), P()),
        check_vma=False,
    )
```

profile of v0, /device:TPU:120, one launch (start us, length us, event | category | flops | bytes accessed | tf_op | source)
XLA Modules:
  0.0 436.7 jit_solution(5991941233304587757)
XLA Ops:
  9.3 1.9 copy.46
  17.9 2.8 collective-permute-done.5
  22.0 3.9 collective-permute-done.6
  25.9 1.5 collective-permute-start.7
  27.5 2.0 collective-permute-done.7
  29.5 21.2 %all-gather.5.cloned.1.call-done = bf16[2,4352,256]{2,1,0:T(8,128)(2,1)} async-done(((bf16[2,272,256]{2,1,0:T(8,128)(2,1)}), bf16[2,4352,256]{2,1,0:T(8,128)(2,1)}) %all-gather.5.cloned.1.call-update) | async-done | bytes 4456464 | tf_op jit(solution)/shard_map/all_gather | solution.py:177
  50.7 3.8 fusion.106
  56.0 2.2 copy-done.2
  59.1 33.8 %all-gather.7.cloned.1.call-done = bf16[2,4352,256]{2,0,1:T(2,128)(2,1)} async-done(((bf16[2,272,256]{2,0,1:T(2,128)(2,1)}), bf16[2,4352,256]{2,0,1:T(2,128)(2,1)}) %all-gather.7.cloned.1.call-update) | async-done | bytes 4456464 | tf_op jit(solution)/shard_map/all_gather | solution.py:178
  92.9 10.2 %fusion.19 = bf16[2,272,256]{2,1,0:T(8,128)(2,1)S(1)} fusion(bf16[2,4352,256]{2,1,0:T(8,128)(2,1)} %all-gather.5.cloned.1.call-done, f32[2,272,4352]{2,1,0:T(8,128)} %copy-done.2, bf16[2,272,256]{2,1,0:T(8,128)(2,1)S(1)} %bitcast.216, f32[2,272]{1,0:T(2,128)S(1)} %copy.64, f32[2,272]{1,0:T(2,128)S(1)} %log_add_fusion, ...), kind=kOutput, calls=%fused_computation.44 | convolution fusion | flops 2434056192 | bytes 18944256 | tf_op jit(solution)/shard_map/shqk,skhd->sqhd/dot_general | solution.py:183
  104.2 2.7 collective-permute-done.1
  107.0 2.2 collective-permute-start.2
  109.2 3.9 collective-permute-done.2
  113.9 4.5 %collective-permute-done.3 = f32[8,2,2,272,1]{3,0,2,4,1:T(8,128)S(1)} collective-permute-done((f32[8,2,2,272,1]{3,0,2,4,1:T(8,128)S(1)}, f32[8,2,2,272,1]{3,0,2,4,1:T(8,128)S(1)}, u32[]{:S(2)}, u32[]{:S(2)}) %collective-permute-start.3) | collective-permute-done | bytes 34848 | tf_op jit(solution)/shard_map/ppermute | solution.py:43
  118.7 17.1 %all-gather.9.cloned.1.call-done = bf16[2,4352,256]{2,1,0:T(8,128)(2,1)} async-done(((bf16[2,272,256]{2,1,0:T(8,128)(2,1)}), bf16[2,4352,256]{2,1,0:T(8,128)(2,1)}) %all-gather.9.cloned.1.call-update) | async-done | bytes 4456464 | tf_op jit(solution)/shard_map/all_gather | solution.py:187
  135.8 7.5 %subtract_exponential_fusion = f32[2,4352,272]{1,2,0:T(8,128)} fusion(bf16[2,4352,256]{2,1,0:T(8,128)(2,1)} %all-gather.9.cloned.1.call-done, f32[2,4352]{1,0:T(2,128)S(1)} %sub.118, bf16[2,272,256]{2,0,1:T(2,128)(2,1)S(1)} %bitcast.218), kind=kOutput, calls=%fused_computation.1 | convolution fusion | flops 1216888832 | bytes 14239744 | tf_op jit(solution)/shard_map/sqhd,skhd->shqk/dot_general | solution.py:143
  143.3 34.9 %all-gather.11.cloned.1.call-done = bf16[2,4352,256]{2,1,0:T(8,128)(2,1)} async-done(((bf16[2,272,256]{2,1,0:T(8,128)(2,1)}), bf16[2,4352,256]{2,1,0:T(8,128)(2,1)}) %all-gather.11.cloned.1.call-update) | async-done | bytes 4456464 | tf_op jit(solution)/shard_map/all_gather | solution.py:188
  178.1 6.3 %fusion.14 = bf16[2,256,272]{1,2,0:T(8,128)(2,1)S(1)} fusion(bf16[2,4352,256]{2,1,0:T(8,128)(2,1)} %all-gather.11.cloned.1.call-done, f32[2,4352,272]{1,2,0:T(8,128)} %subtract_exponential_fusion), kind=kOutput, calls=%fused_computation.40 | convolution fusion | flops 1214660608 | bytes 14204928 | tf_op jit(solution)/shard_map/shqk,sqhd->skhd/dot_general | solution.py:196
  184.5 9.0 %fusion.13 = bf16[2,272,256]{2,1,0:T(8,128)(2,1)S(1)} fusion(bf16[2,4352,256]{2,1,0:T(8,128)(2,1)} %all-gather.9.cloned.1.call-done, f32[2,4352,272]{1,2,0:T(8,128)} %subtract_exponential_fusion, bf16[2,4352,256]{2,1,0:T(8,128)(2,1)} %all-gather.11.cloned.1.call-done, f32[2,4352]{1,0:T(2,128)S(1)} %sub.121, bf16[2,272,256]{2,0,1:T(2,128)(2,1)S(1)} %bitcast.220), kind=kOutput, calls=%fused_computation.39 | convolution fusion | flops 2431688704 | bytes 18974720 | tf_op jit(solution)/shard_map/shqk,sqhd->skhd/dot_general | solution.py:195
  194.0 2.1 collective-permute-start.8
  196.1 3.6 collective-permute-start.9
  204.3 1.7 reshape.731
  206.0 1.7 reshape.730
  217.5 1.9 multiply_reduce_fusion
  219.3 6.3 %collective-permute-start.14 = (bf16[2,1,68,256]{3,2,1,0:T(8,128)(2,1)S(1)}, bf16[2,1,68,256]{3,2,1,0:T(8,128)(2,1)S(1)}, u32[]{:S(2)}, u32[]{:S(2)}) collective-permute-start(bf16[2,1,68,256]{3,2,1,0:T(8,128)(2,1)S(1)} %get-tuple-element.41), channel_id=1, source_target_pairs={{0,1},{1,2},{2,3},{3,4},{4,5},{5,6},{6,7},{7,8},{8,9},{9,10},{10,1... | collective-permute-start | bytes 208904 | tf_op jit(solution)/shard_map/ppermute | solution.py:19
  225.6 1.9 collective-permute-start.15
  236.8 2.1 convolution_add_fusion.7
  244.4 3.0 fusion.22
  248.7 2.0 fusion.30
  257.8 3.0 copy.67
  261.8 1.5 fusion.6
  264.1 3.9 collective-permute-start.16
  268.1 3.7 collective-permute-done.16
  271.7 2.2 select_add_fusion
  275.4 13.0 %collective-permute-done.17 = f32[221184]{0:T(1024)S(1)} collective-permute-done((f32[221184]{0:T(1024)S(1)}, f32[221184]{0:T(1024)S(1)}, u32[]{:S(2)}, u32[]{:S(2)}) %collective-permute-start.17) | collective-permute-done | bytes 884768 | tf_op jit(solution)/shard_map/ppermute | solution.py:71
  288.4 1.6 select_add_fusion.1
  290.1 8.3 %collective-permute-done.18 = f32[110592]{0:T(1024)S(1)} collective-permute-done((f32[110592]{0:T(1024)S(1)}, f32[110592]{0:T(1024)S(1)}, u32[]{:S(2)}, u32[]{:S(2)}) %collective-permute-start.18) | collective-permute-done | bytes 442400 | tf_op jit(solution)/shard_map/ppermute | solution.py:71
  299.3 5.5 %collective-permute-done.19 = f32[55296]{0:T(1024)S(1)} collective-permute-done((f32[55296]{0:T(1024)S(1)}, f32[55296]{0:T(1024)S(1)}, u32[]{:S(2)}, u32[]{:S(2)}) %collective-permute-start.19) | collective-permute-done | bytes 221216 | tf_op jit(solution)/shard_map/ppermute | solution.py:71
  304.9 6.2 %collective-permute-done.20 = f32[27648]{0:T(1024)S(1)} collective-permute-done((f32[27648]{0:T(1024)S(1)}, f32[27648]{0:T(1024)S(1)}, u32[]{:S(2)}, u32[]{:S(2)}) %collective-permute-start.20) | collective-permute-done | bytes 110624 | tf_op jit(solution)/shard_map/ppermute | solution.py:71
  311.2 2.8 collective-permute-start.21
  314.0 3.0 collective-permute-done.21
  317.7 4.4 %collective-permute-done.22 = f32[6912]{0:T(1024)S(1)} collective-permute-done((f32[6912]{0:T(1024)S(1)}, f32[6912]{0:T(1024)S(1)}, u32[]{:S(2)}, u32[]{:S(2)}) %collective-permute-start.22) | collective-permute-done | bytes 27680 | tf_op jit(solution)/shard_map/ppermute | solution.py:71
  322.2 2.8 collective-permute-start.23
  325.0 4.9 %collective-permute-done.23 = f32[3456]{0:T(1024)S(1)} collective-permute-done((f32[3456]{0:T(1024)S(1)}, f32[3456]{0:T(1024)S(1)}, u32[]{:S(2)}, u32[]{:S(2)}) %collective-permute-start.23) | collective-permute-done | bytes 13856 | tf_op jit(solution)/shard_map/ppermute | solution.py:71
  329.9 2.7 collective-permute-start.24
  332.6 4.9 %collective-permute-done.24 = f32[3456]{0:T(1024)S(1)} collective-permute-done((f32[3456]{0:T(1024)S(1)}, f32[3456]{0:T(1024)S(1)}, u32[]{:S(2)}, u32[]{:S(2)}) %collective-permute-start.24) | collective-permute-done | bytes 13856 | tf_op jit(solution)/shard_map/ppermute | solution.py:74
  338.0 6.0 %collective-permute-done.25 = f32[6912]{0:T(1024)S(1)} collective-permute-done((f32[6912]{0:T(1024)S(1)}, f32[6912]{0:T(1024)S(1)}, u32[]{:S(2)}, u32[]{:S(2)}) %collective-permute-start.25) | collective-permute-done | bytes 27680 | tf_op jit(solution)/shard_map/ppermute | solution.py:74
  344.0 2.8 collective-permute-start.26
  346.8 3.6 collective-permute-done.26
  350.5 7.4 %collective-permute-done.27 = f32[27648]{0:T(1024)S(1)} collective-permute-done((f32[27648]{0:T(1024)S(1)}, f32[27648]{0:T(1024)S(1)}, u32[]{:S(2)}, u32[]{:S(2)}) %collective-permute-start.27) | collective-permute-done | bytes 110624 | tf_op jit(solution)/shard_map/ppermute | solution.py:74
  358.0 8.3 %collective-permute-done.28 = f32[55296]{0:T(1024)S(1)} collective-permute-done((f32[55296]{0:T(1024)S(1)}, f32[55296]{0:T(1024)S(1)}, u32[]{:S(2)}, u32[]{:S(2)}) %collective-permute-start.28) | collective-permute-done | bytes 221216 | tf_op jit(solution)/shard_map/ppermute | solution.py:74
  367.0 7.8 %collective-permute-done.29 = f32[110592]{0:T(1024)S(1)} collective-permute-done((f32[110592]{0:T(1024)S(1)}, f32[110592]{0:T(1024)S(1)}, u32[]{:S(2)}, u32[]{:S(2)}) %collective-permute-start.29) | collective-permute-done | bytes 442400 | tf_op jit(solution)/shard_map/ppermute | solution.py:74
  375.5 13.0 %collective-permute-done.30 = f32[221184]{0:T(1024)S(1)} collective-permute-done((f32[221184]{0:T(1024)S(1)}, f32[221184]{0:T(1024)S(1)}, u32[]{:S(2)}, u32[]{:S(2)}) %collective-permute-start.30) | collective-permute-done | bytes 884768 | tf_op jit(solution)/shard_map/ppermute | solution.py:74
  391.0 2.9 collective-permute-done.10
  393.9 3.6 collective-permute-done.11
  397.5 5.1 %collective-permute-done.12 = f32[2,2,32]{2,1,0:T(2,128)S(1)} collective-permute-done((f32[2,2,32]{2,1,0:T(2,128)S(1)}, f32[2,2,32]{2,1,0:T(2,128)S(1)}, u32[]{:S(2)}, u32[]{:S(2)}) %collective-permute-start.12) | collective-permute-done | bytes 544 | tf_op jit(solution)/shard_map/ppermute | solution.py:32
  402.8 3.6 collective-permute-done.13
  410.7 1.9 concatenate.347
  412.7 2.5 maximum_select_fusion.4
  416.3 3.5 maximum_select_fusion.2
  419.7 3.0 maximum_select_fusion
  423.6 1.8 reshape.748
  426.3 1.8 concatenate.345
  428.2 1.7 fusion.37
  (266 shorter events, 69.1 us)
Async XLA Ops:
  7.2 186.3 %copy-start = (bf16[256,768]{1,0:T(8,128)(2,1)S(1)}, bf16[256,768]{1,0:T(8,128)(2,1)}, u32[]{:S(2)}) copy-start(bf16[256,768]{1,0:T(8,128)(2,1)} %param.18) | copy-start | bytes 1179652
  7.2 4.2 copy-start.30
  7.2 5.2 %copy-start.31 = (bf16[2,4,68,256]{3,1,2,0:T(4,128)(2,1)S(1)}, bf16[2,4,68,256]{3,1,2,0:T(4,128)(2,1)}, u32[]{:S(2)}) copy-start(bf16[2,4,68,256]{3,1,2,0:T(4,128)(2,1)} %param.16) | copy-start | bytes 835588
  7.2 5.3 %copy-start.35 = (bf16[256,256]{1,0:T(8,128)(2,1)S(1)}, bf16[256,256]{1,0:T(8,128)(2,1)}, u32[]{:S(2)}) copy-start(bf16[256,256]{1,0:T(8,128)(2,1)} %param.19) | copy-start | bytes 393220
  7.2 43.5 %all-gather.5.cloned.1.call-start = ((), (), s32[]{:S(2)}) async-start(), calls=%async_computation | async-start | bytes 4734976 | tf_op jit(solution)/shard_map/all_gather | solution.py:177
  9.2 4.3 copy-start.7
  9.3 83.6 %all-gather.7.cloned.1.call-start = ((), (), s32[]{:S(2)}) async-start(), calls=%async_computation.1 | async-start | bytes 4734976 | tf_op jit(solution)/shard_map/all_gather | solution.py:178
  11.3 3.9 copy-start.32
  11.3 124.5 %all-gather.9.cloned.1.call-start = ((), (), s32[]{:S(2)}) async-start(), calls=%async_computation.2 | async-start | bytes 4734976 | tf_op jit(solution)/shard_map/all_gather | solution.py:187
  12.3 165.8 %all-gather.11.cloned.1.call-start = ((), (), s32[]{:S(2)}) async-start(), calls=%async_computation.3 | async-start | bytes 4734976 | tf_op jit(solution)/shard_map/all_gather | solution.py:188
  14.0 3.1 collective-permute-start.4
  15.8 38.7 %copy-start.10 = (f32[32,2,8,128]{3,1,2,0:T(2,128)}, f32[32,2,8,128]{3,1,2,0:T(2,128)S(1)}, u32[]{:S(2)}) copy-start(f32[32,2,8,128]{3,1,2,0:T(2,128)S(1)} %copy.66) | copy-start | bytes 786436
  17.1 3.7 collective-permute-start.5
  20.8 5.1 %collective-permute-start.6 = (f32[2,2,32]{2,1,0:T(2,128)S(1)}, f32[2,2,32]{2,1,0:T(2,128)S(1)}, u32[]{:S(2)}, u32[]{:S(2)}) collective-permute-start(f32[2,2,32]{2,1,0:T(2,128)S(1)} %fusion.154), channel_id=1, source_target_pairs={{0,4},{1,5},{2,6},{3,7},{4,0},{5,1},{6,2},{7,3},{8,12},{9,13},{10,... | collective-permute-start | bytes 1544 | tf_op jit(solution)/shard_map/ppermute | solution.py:32
  25.9 3.6 collective-permute-start.7
  54.5 3.7 copy-start.2
  54.6 38.3 %copy-start.12 = (bf16[544,256]{1,0:T(8,128)(2,1)S(1)}, bf16[544,256]{1,0:T(8,128)(2,1)}, u32[]{:S(2)}) copy-start(bf16[544,256]{1,0:T(8,128)(2,1)} %convolution_convert_fusion) | copy-start | bytes 835588
  58.3 44.9 %collective-permute-start = (f32[1,2,2,272,1]{3,4,2,1,0:T(1,128)S(1)}, f32[1,2,2,272,1]{3,4,2,1,0:T(1,128)S(1)}, u32[]{:S(2)}, u32[]{:S(2)}) collective-permute-start(f32[1,2,2,272,1]{3,4,2,1,0:T(1,128)S(1)} %get-tuple-element.50), channel_id=1, source_target_pairs={{0,1},{1,0},{2,3},{3,2},{4,5},{5,4},{6,7},{7,6},{8,9},{9,8},{10,11... | collective-permute-start | bytes 13064 | tf_op jit(solution)/shard_map/ppermute | solution.py:43
  103.1 90.4 %copy-start.40 = (bf16[2,272,256]{2,1,0:T(8,128)(2,1)}, bf16[2,272,256]{2,1,0:T(8,128)(2,1)S(1)}, u32[]{:S(2)}) copy-start(bf16[2,272,256]{2,1,0:T(8,128)(2,1)S(1)} %fusion.19) | copy-start | bytes 835588
  103.2 3.8 collective-permute-start.1
  107.0 6.1 %collective-permute-start.2 = (f32[4,2,2,272,1]{3,0,2,1,4:T(4,128)S(1)}, f32[4,2,2,272,1]{3,0,2,1,4:T(4,128)S(1)}, u32[]{:S(2)}, u32[]{:S(2)}) collective-permute-start(f32[4,2,2,272,1]{3,0,2,1,4:T(4,128)S(1)} %maximum_select_fusion.14), channel_id=1, source_target_pairs={{0,4},{1,5},{2,6},{3,7},{4,0},{5,1},{6,2},{7,3},{8,12},{9,13},{10,... | collective-permute-start | bytes 52232 | tf_op jit(solution)/shard_map/ppermute | solution.py:43
  113.1 5.3 %collective-permute-start.3 = (f32[8,2,2,272,1]{3,0,2,4,1:T(8,128)S(1)}, f32[8,2,2,272,1]{3,0,2,4,1:T(8,128)S(1)}, u32[]{:S(2)}, u32[]{:S(2)}) collective-permute-start(f32[8,2,2,272,1]{3,0,2,4,1:T(8,128)S(1)} %fusion.81), channel_id=1, source_target_pairs={{0,8},{1,9},{2,10},{3,11},{4,12},{5,13},{6,14},{7,15},{8,0},{9,1},... | collective-permute-start | bytes 104456 | tf_op jit(solution)/shard_map/ppermute | solution.py:43
  143.3 41.2 %copy-start.19 = (bf16[2,4,68,256]{3,0,2,1:T(2,128)(2,1)S(1)}, bf16[2,4,68,256]{3,0,2,1:T(2,128)(2,1)}, u32[]{:S(2)}) copy-start(bf16[2,4,68,256]{3,0,2,1:T(2,128)(2,1)} %copy.46) | copy-start | bytes 835588
  184.5 9.0 %copy-start.28 = (bf16[2,256,272]{1,2,0:T(8,128)(2,1)}, bf16[2,256,272]{1,2,0:T(8,128)(2,1)S(1)}, u32[]{:S(2)}) copy-start(bf16[2,256,272]{1,2,0:T(8,128)(2,1)S(1)} %fusion.14) | copy-start | bytes 835588
  193.5 8.1 %copy-start.33 = (bf16[2,272,256]{2,1,0:T(8,128)(2,1)}, bf16[2,272,256]{2,1,0:T(8,128)(2,1)S(1)}, u32[]{:S(2)}) copy-start(bf16[2,272,256]{2,1,0:T(8,128)(2,1)S(1)} %fusion.13) | copy-start | bytes 835588
  194.0 6.1 %collective-permute-start.8 = (bf16[2,1,68,256]{3,2,1,0:T(8,128)(2,1)S(1)}, bf16[2,1,68,256]{3,2,1,0:T(8,128)(2,1)S(1)}, u32[]{:S(2)}, u32[]{:S(2)}) collective-permute-start(bf16[2,1,68,256]{3,2,1,0:T(8,128)(2,1)S(1)} %get-tuple-element.45), channel_id=1, source_target_pairs={{0,1},{1,2},{2,3},{3,4},{4,5},{5,6},{6,7},{7,8},{8,9},{9,10},{10,1... | collective-permute-start | bytes 208904 | tf_op jit(solution)/shard_map/ppermute | solution.py:19
  196.1 5.4 %collective-permute-start.9 = (bf16[2,1,68,256]{3,2,1,0:T(8,128)(2,1)S(1)}, bf16[2,1,68,256]{3,2,1,0:T(8,128)(2,1)S(1)}, u32[]{:S(2)}, u32[]{:S(2)}) collective-permute-start(bf16[2,1,68,256]{3,2,1,0:T(8,128)(2,1)S(1)} %get-tuple-element.46), channel_id=1, source_target_pairs={{1,0},{2,1},{3,2},{4,3},{5,4},{6,5},{7,6},{8,7},{9,8},{10,9},{11,1... | collective-permute-start | bytes 208904 | tf_op jit(solution)/shard_map/ppermute | solution.py:21
  203.3 6.0 %copy-start.9 = (bf16[9,256,256]{2,1,0:T(8,128)(2,1)S(1)}, bf16[9,256,256]{2,1,0:T(8,128)(2,1)}, u32[]{:S(2)}) copy-start(bf16[9,256,256]{2,1,0:T(8,128)(2,1)} %param.17) | copy-start | bytes 3538948
  208.6 3.5 copy-start.25
  219.3 9.2 %collective-permute-start.14 = (bf16[2,1,68,256]{3,2,1,0:T(8,128)(2,1)S(1)}, bf16[2,1,68,256]{3,2,1,0:T(8,128)(2,1)S(1)}, u32[]{:S(2)}, u32[]{:S(2)}) collective-permute-start(bf16[2,1,68,256]{3,2,1,0:T(8,128)(2,1)S(1)} %get-tuple-element.41), channel_id=1, source_target_pairs={{0,1},{1,2},{2,3},{3,4},{4,5},{5,6},{6,7},{7,8},{8,9},{9,10},{10,1... | collective-permute-start | bytes 208904 | tf_op jit(solution)/shard_map/ppermute | solution.py:19
  225.6 3.9 collective-permute-start.15
  233.5 9.1 %copy-start.15 = (bf16[544,256]{1,0:T(8,128)(2,1)}, bf16[544,256]{1,0:T(8,128)(2,1)S(1)}, u32[]{:S(2)}) copy-start(bf16[544,256]{1,0:T(8,128)(2,1)S(1)} %reshape.740) | copy-start | bytes 835588
  234.6 6.5 %copy-start.17 = (bf16[544,256]{1,0:T(8,128)(2,1)}, bf16[544,256]{1,0:T(8,128)(2,1)S(1)}, u32[]{:S(2)}) copy-start(bf16[544,256]{1,0:T(8,128)(2,1)S(1)} %reshape.739) | copy-start | bytes 835588
  239.9 3.0 copy-start.13
  247.4 3.3 copy-start.18
  247.4 4.3 copy-start.16
  248.7 7.1 %copy-start.22 = (bf16[544,256]{1,0:T(8,128)(2,1)S(1)}, bf16[544,256]{1,0:T(8,128)(2,1)}, u32[]{:S(2)}) copy-start(bf16[544,256]{1,0:T(8,128)(2,1)} %reshape.744) | copy-start | bytes 835588
  250.7 6.1 %copy-start.14 = (bf16[544,256]{1,0:T(8,128)(2,1)S(1)}, bf16[544,256]{1,0:T(8,128)(2,1)}, u32[]{:S(2)}) copy-start(bf16[544,256]{1,0:T(8,128)(2,1)} %copy-done.13) | copy-start | bytes 835588
  257.8 3.0 copy-start.4
  264.1 7.6 %collective-permute-start.16 = (f32[442368]{0:T(1024)}, f32[442368]{0:T(1024)}, u32[]{:S(2)}, u32[]{:S(2)}) collective-permute-start(f32[442368]{0:T(1024)} %fusion.6), channel_id=1, source_target_pairs={{0,1},{1,0},{2,3},{3,2},{4,5},{5,4},{6,7},{7,6},{8,9},{9,8},{10,11... | collective-permute-start | bytes 5308424 | tf_op jit(solution)/shard_map/ppermute | solution.py:71
  275.3 13.1 %collective-permute-start.17 = (f32[221184]{0:T(1024)S(1)}, f32[221184]{0:T(1024)S(1)}, u32[]{:S(2)}, u32[]{:S(2)}) collective-permute-start(f32[221184]{0:T(1024)S(1)} %slice_select_fusion), channel_id=1, source_target_pairs={{0,2},{1,17},{2,0},{3,19},{4,6},{5,21},{6,4},{7,23},{8,10},{9,25},... | collective-permute-start | bytes 2654216 | tf_op jit(solution)/shard_map/ppermute | solution.py:71
  290.0 8.4 %collective-permute-start.18 = (f32[110592]{0:T(1024)S(1)}, f32[110592]{0:T(1024)S(1)}, u32[]{:S(2)}, u32[]{:S(2)}) collective-permute-start(f32[110592]{0:T(1024)S(1)} %slice_select_fusion.1), channel_id=1, source_target_pairs={{0,8},{1,3},{2,10},{3,1},{4,12},{5,7},{6,14},{7,5},{8,0},{9,11},{1... | collective-permute-start | bytes 1327112 | tf_op jit(solution)/shard_map/ppermute | solution.py:71
  298.5 6.2 %collective-permute-start.19 = (f32[55296]{0:T(1024)S(1)}, f32[55296]{0:T(1024)S(1)}, u32[]{:S(2)}, u32[]{:S(2)}) collective-permute-start(f32[55296]{0:T(1024)S(1)} %slice_select_fusion.2), channel_id=1, source_target_pairs={{0,16},{1,9},{2,18},{3,11},{4,20},{5,13},{6,22},{7,15},{8,24},{9,1... | collective-permute-start | bytes 663560 | tf_op jit(solution)/shard_map/ppermute | solution.py:71
  304.8 6.3 %collective-permute-start.20 = (f32[27648]{0:T(1024)S(1)}, f32[27648]{0:T(1024)S(1)}, u32[]{:S(2)}, u32[]{:S(2)}) collective-permute-start(f32[27648]{0:T(1024)S(1)} %slice_select_fusion.3), channel_id=1, source_target_pairs={{0,4},{1,33},{2,6},{3,35},{4,0},{5,37},{6,2},{7,39},{8,12},{9,41},... | collective-permute-start | bytes 331784 | tf_op jit(solution)/shard_map/ppermute | solution.py:71
  311.2 5.8 %collective-permute-start.21 = (f32[13824]{0:T(1024)S(1)}, f32[13824]{0:T(1024)S(1)}, u32[]{:S(2)}, u32[]{:S(2)}) collective-permute-start(f32[13824]{0:T(1024)S(1)} %slice_select_fusion.4), channel_id=1, source_target_pairs={{0,128},{1,5},{2,130},{3,7},{4,132},{5,1},{6,134},{7,3},{8,136},{9... | collective-permute-start | bytes 165896 | tf_op jit(solution)/shard_map/ppermute | solution.py:71
  317.0 5.2 %collective-permute-start.22 = (f32[6912]{0:T(1024)S(1)}, f32[6912]{0:T(1024)S(1)}, u32[]{:S(2)}, u32[]{:S(2)}) collective-permute-start(f32[6912]{0:T(1024)S(1)} %slice_select_fusion.5), channel_id=1, source_target_pairs={{0,32},{1,129},{2,34},{3,131},{4,36},{5,133},{6,38},{7,135},{8,40}... | collective-permute-start | bytes 82952 | tf_op jit(solution)/shard_map/ppermute | solution.py:71
  322.2 7.7 %collective-permute-start.23 = (f32[3456]{0:T(1024)S(1)}, f32[3456]{0:T(1024)S(1)}, u32[]{:S(2)}, u32[]{:S(2)}) collective-permute-start(f32[3456]{0:T(1024)S(1)} %slice_select_fusion.6), channel_id=1, source_target_pairs={{0,64},{1,65},{2,66},{3,67},{4,68},{5,69},{6,70},{7,71},{8,72},{9,... | collective-permute-start | bytes 41480 | tf_op jit(solution)/shard_map/ppermute | solution.py:71
  329.9 7.6 %collective-permute-start.24 = (f32[3456]{0:T(1024)S(1)}, f32[3456]{0:T(1024)S(1)}, u32[]{:S(2)}, u32[]{:S(2)}) collective-permute-start(f32[3456]{0:T(1024)S(1)} %select_add_fusion.7), channel_id=1, source_target_pairs={{0,64},{1,65},{2,66},{3,67},{4,68},{5,69},{6,70},{7,71},{8,72},{9,... | collective-permute-start | bytes 41480 | tf_op jit(solution)/shard_map/ppermute | solution.py:74
  337.6 6.4 %collective-permute-start.25 = (f32[6912]{0:T(1024)S(1)}, f32[6912]{0:T(1024)S(1)}, u32[]{:S(2)}, u32[]{:S(2)}) collective-permute-start(f32[6912]{0:T(1024)S(1)} %maximum_select_fusion.13), channel_id=1, source_target_pairs={{0,32},{1,129},{2,34},{3,131},{4,36},{5,133},{6,38},{7,135},{8,40}... | collective-permute-start | bytes 82952 | tf_op jit(solution)/shard_map/ppermute | solution.py:74
  344.0 6.4 %collective-permute-start.26 = (f32[13824]{0:T(1024)S(1)}, f32[13824]{0:T(1024)S(1)}, u32[]{:S(2)}, u32[]{:S(2)}) collective-permute-start(f32[13824]{0:T(1024)S(1)} %maximum_select_fusion.10), channel_id=1, source_target_pairs={{0,128},{1,5},{2,130},{3,7},{4,132},{5,1},{6,134},{7,3},{8,136},{9... | collective-permute-start | bytes 165896 | tf_op jit(solution)/shard_map/ppermute | solution.py:74
  350.4 7.5 %collective-permute-start.27 = (f32[27648]{0:T(1024)S(1)}, f32[27648]{0:T(1024)S(1)}, u32[]{:S(2)}, u32[]{:S(2)}) collective-permute-start(f32[27648]{0:T(1024)S(1)} %maximum_select_fusion.8), channel_id=1, source_target_pairs={{0,4},{1,33},{2,6},{3,35},{4,0},{5,37},{6,2},{7,39},{8,12},{9,41},... | collective-permute-start | bytes 331784 | tf_op jit(solution)/shard_map/ppermute | solution.py:74
  357.9 8.4 %collective-permute-start.28 = (f32[55296]{0:T(1024)S(1)}, f32[55296]{0:T(1024)S(1)}, u32[]{:S(2)}, u32[]{:S(2)}) collective-permute-start(f32[55296]{0:T(1024)S(1)} %maximum_select_fusion.7), channel_id=1, source_target_pairs={{0,16},{1,9},{2,18},{3,11},{4,20},{5,13},{6,22},{7,15},{8,24},{9,1... | collective-permute-start | bytes 663560 | tf_op jit(solution)/shard_map/ppermute | solution.py:74
  366.4 23.8 %copy-start.36 = (f32[2,256]{1,0:T(2,128)S(1)}, f32[2,256]{1,0:T(2,128)}, u32[]{:S(2)}) copy-start(f32[2,256]{1,0:T(2,128)} %get-tuple-element.20) | copy-start | bytes 6148
  366.4 8.4 %collective-permute-start.29 = (f32[110592]{0:T(1024)S(1)}, f32[110592]{0:T(1024)S(1)}, u32[]{:S(2)}, u32[]{:S(2)}) collective-permute-start(f32[110592]{0:T(1024)S(1)} %maximum_select_fusion.5), channel_id=1, source_target_pairs={{0,8},{1,3},{2,10},{3,1},{4,12},{5,7},{6,14},{7,5},{8,0},{9,11},{1... | collective-permute-start | bytes 1327112 | tf_op jit(solution)/shard_map/ppermute | solution.py:74
  375.5 31.2 %copy-start.8 = (bf16[2,4,68,256]{3,1,2,0:T(4,128)(2,1)S(1)}, bf16[2,4,68,256]{3,1,2,0:T(4,128)(2,1)}, u32[]{:S(2)}) copy-start(bf16[2,4,68,256]{3,1,2,0:T(4,128)(2,1)} %param.11) | copy-start | bytes 835588
  375.5 31.2 %copy-start.38 = (f32[256]{0:T(256)S(1)}, f32[256]{0:T(256)}, u32[]{:S(2)}) copy-start(f32[256]{0:T(256)} %param.20) | copy-start | bytes 3076
  375.5 13.0 %collective-permute-start.30 = (f32[221184]{0:T(1024)S(1)}, f32[221184]{0:T(1024)S(1)}, u32[]{:S(2)}, u32[]{:S(2)}) collective-permute-start(f32[221184]{0:T(1024)S(1)} %maximum_select_fusion.3), channel_id=1, source_target_pairs={{0,2},{1,17},{2,0},{3,19},{4,6},{5,21},{6,4},{7,23},{8,10},{9,25},... | collective-permute-start | bytes 2654216 | tf_op jit(solution)/shard_map/ppermute | solution.py:74
  390.0 29.8 %collective-permute-start.31 = (f32[442368]{0:T(1024)}, f32[442368]{0:T(1024)S(1)}, u32[]{:S(2)}, u32[]{:S(2)}) collective-permute-start(f32[442368]{0:T(1024)} %maximum_select_fusion.1), channel_id=1, source_target_pairs={{0,1},{1,0},{2,3},{3,2},{4,5},{5,4},{6,7},{7,6},{8,9},{9,8},{10,11... | collective-permute-start | bytes 5308424 | tf_op jit(solution)/shard_map/ppermute | solution.py:74
  390.4 3.5 collective-permute-start.10
  393.9 3.6 collective-permute-start.11
  397.5 5.1 %collective-permute-start.12 = (f32[2,2,32]{2,1,0:T(2,128)S(1)}, f32[2,2,32]{2,1,0:T(2,128)S(1)}, u32[]{:S(2)}, u32[]{:S(2)}) collective-permute-start(f32[2,2,32]{2,1,0:T(2,128)S(1)} %fusion.153), channel_id=1, source_target_pairs={{0,4},{1,5},{2,6},{3,7},{4,0},{5,1},{6,2},{7,3},{8,12},{9,13},{10,... | collective-permute-start | bytes 1544 | tf_op jit(solution)/shard_map/ppermute | solution.py:32
  402.6 3.8 collective-permute-start.13
  419.7 3.0 copy-start.6
  426.3 3.5 copy-start.1
  (13 other events, 22.4 us)
Sparse Core Ops, SparseCore 0:
  10.4 40.2 all-gather.4
  52.6 40.2 all-gather.6
  95.3 40.4 all-gather.8
  138.0 40.0 all-gather.10
where the time goes:
time: 444 us; the launch traced here: 437 us
  waiting for transfers between devices  244 us (55%)
  matrix products  64.2 us (14%)
  local copies, waits for them, and re-layouts  46 us (10%)
  starting transfers between devices  40.9 us (9%)
  other arithmetic  26 us (6%)
  between operations  15.3 us (3%)
    ppermute x8, waiting for transfers between devices, mesh_psum(): got = lax.ppermute(values, MESH_AXES, pairs)  51 us
    ppermute x8, waiting for transfers between devices, mesh_psum(): values = keep + lax.ppermute(send, MESH_AXES, pairs)  49 us
    all_gather x1, waiting for transfers between devices, body(): lax.all_gather(do_rows, 'dom', axis=1, tiled=True)  34.9 us
    all_gather x1, waiting for transfers between devices, body(): lax.all_gather(v_rows, 'dom', axis=1, tiled=True)  33.8 us
    ppermute x8, waiting for transfers between devices, dom_psum(): lax.ppermute(values, 'dom', [(i, i ^ step) for i in range(count)])  23.9 us
    all_gather x1, waiting for transfers between devices, body(): lax.all_gather(k_rows, 'dom', axis=1, tiled=True)  21.2 us
    all_gather x1, waiting for transfers between devices, body(): lax.all_gather(q_rows, 'dom', axis=1, tiled=True)  17.1 us
    unnamed x94, local copies, waits for them, and re-layouts  14.9 us
  transfers between devices with their start and end apart: 36, of which 31 were waited for; matrix products, arithmetic and copies ran while one was open for 10% of the time, Pallas kernels for 0%

commit v1 on v0

--- a/solution.py
+++ b/solution.py
@@ -185,7 +185,15 @@
     stats_all = stats_local.transpose(1, 2, 0, 3, 4).reshape(2, samples, -1, HEADS)
     shard_piece = (
         lax.all_gather(q_rows, "dom", axis=1, tiled=True),
-        lax.all_gather(do_rows, "dom", axis=1, tiled=True),
+        jnp.concatenate(
+            lax.all_to_all(
+                jnp.stack([do_rows for _ in range(lax.axis_size("dom"))], axis=0),
+                "dom",
+                split_axis=0,
+                concat_axis=0,
+            ),
+            axis=1,
+        ),
     )
     query_heads = split_heads(shard_piece[0])
     dout_heads = split_heads(shard_piece[1])

time: 444 us -> 457 us (1.029)
  local copies, waits for them, and re-layouts: 46 us -> 56.9 us
  matrix products: 64.2 us -> 57 us
  waiting for transfers between devices: 244 us -> 251 us
    ppermute x8, waiting for transfers between devices: 23.9 us -> 94.1 us  [dom_psum(): lax.ppermute(values, 'dom', [(i, i ^ step) for i in range(count)])]
    all_gather x1 -> x0, waiting for transfers between devices: 34.9 us -> none  [body(): lax.all_gather(do_rows, 'dom', axis=1, tiled=True)]
    all_gather x1, waiting for transfers between devices: 21.2 us -> 0.01 us  [body(): lax.all_gather(k_rows, 'dom', axis=1, tiled=True)]
    all_gather x1, waiting for transfers between devices: 33.8 us -> 25.7 us  [body(): lax.all_gather(v_rows, 'dom', axis=1, tiled=True)]
    all_to_all x0 -> x1, starting transfers between devices: none -> 5.76 us  [body(): lax.all_to_all(jnp.stack([do_rows for _ in range(lax.axis_size('dom'))],...]
    reshape x1 -> x2, local copies, waits for them, and re-layouts: 0.74 us -> 5.45 us  [the longest x1 4.71 us: body(): jnp.concatenate(lax.all_to_all(jnp.stack([do_rows for _ in range(lax.axis...]
  transfers between devices with their start and end apart: 36 -> 36, of which waited for: 31 -> 29; matrix products, arithmetic and copies ran while one was open for 10% -> 10% of each run, Pallas kernels for 0% -> 0%
where the time goes in v1:
time: 457 us; the launch traced here: 449 us
  waiting for transfers between devices  251 us (55%)
  matrix products  57 us (12%)
  local copies, waits for them, and re-layouts  56.9 us (12%)
  starting transfers between devices  44.5 us (10%)
  other arithmetic  25 us (5%)
  between operations  15.2 us (3%)
    ppermute x8, waiting for transfers between devices, dom_psum(): lax.ppermute(values, 'dom', [(i, i ^ step) for i in range(count)])  94.1 us
    ppermute x8, waiting for transfers between devices, mesh_psum(): got = lax.ppermute(values, MESH_AXES, pairs)  51 us
    ppermute x8, waiting for transfers between devices, mesh_psum(): values = keep + lax.ppermute(send, MESH_AXES, pairs)  49 us
    all_gather x1, waiting for transfers between devices, body(): lax.all_gather(v_rows, 'dom', axis=1, tiled=True)  25.7 us
    unnamed x94, local copies, waits for them, and re-layouts  18.5 us
    all_gather x1, waiting for transfers between devices, body(): lax.all_gather(q_rows, 'dom', axis=1, tiled=True)  17.4 us
    reshape x17, local copies, waits for them, and re-layouts, shifted(): return source[:, row_start:row_start + row_count, col_start:col_start + c...  13.3 us
    select_n x12, other arithmetic, mesh_psum(): jnp.where(upper, jnp.concatenate([got, values]), jnp.concatenate([values,...  13 us
  transfers between devices with their start and end apart: 36, of which 29 were waited for; matrix products, arithmetic and copies ran while one was open for 10% of the time, Pallas kernels for 0%

profile of v1, /device:TPU:120, one launch (start us, length us, event | category | flops | bytes accessed | tf_op | source)
XLA Modules:
  0.0 449.3 jit_solution(17334134595304503945)
XLA Ops:
  9.3 1.9 copy.46
  12.7 2.6 stack.59
  15.2 5.8 %all-to-all-start = ((bf16[16,2,272,256]{3,2,1,0:T(8,128)(2,1)}), bf16[16,2,272,256]{3,2,1,0:T(8,128)(2,1)}, u32[]{:S(2)}, u32[]{:S(2)}) async-start(bf16[16,2,272,256]{3,2,1,0:T(8,128)(2,1)} %stack.59), calls=%async_computation | async-start | bytes 8912896 | tf_op jit(solution)/shard_map/all_to_all | solution.py:189
  24.6 71.0 %collective-permute-done.5 = f32[2,2,32]{2,1,0:T(2,128)S(1)} collective-permute-done((f32[2,2,32]{2,1,0:T(2,128)S(1)}, f32[2,2,32]{2,1,0:T(2,128)S(1)}, u32[]{:S(2)}, u32[]{:S(2)}) %collective-permute-start.5) | collective-permute-done | bytes 544 | tf_op jit(solution)/shard_map/ppermute | solution.py:32
  95.7 5.1 %collective-permute-done.6 = f32[2,2,32]{2,1,0:T(2,128)S(1)} collective-permute-done((f32[2,2,32]{2,1,0:T(2,128)S(1)}, f32[2,2,32]{2,1,0:T(2,128)S(1)}, u32[]{:S(2)}, u32[]{:S(2)}) %collective-permute-start.6) | collective-permute-done | bytes 544 | tf_op jit(solution)/shard_map/ppermute | solution.py:32
  101.5 2.9 collective-permute-done.7
  104.3 4.7 %copy.55 = bf16[2,16,272,256]{3,2,1,0:T(8,128)(2,1)} copy(bf16[2,16,272,256]{3,2,0,1:T(8,128)(2,1)} %bitcast.20) | data formatting | bytes 8912896 | tf_op jit(solution)/shard_map/reshape | solution.py:188
  109.1 3.8 fusion.106
  114.3 2.2 copy-done.3
  117.2 25.7 %all-gather.6.cloned.1.call-done = bf16[2,4352,256]{2,0,1:T(2,128)(2,1)} async-done(((bf16[2,272,256]{2,0,1:T(2,128)(2,1)}), bf16[2,4352,256]{2,0,1:T(2,128)(2,1)}) %all-gather.6.cloned.1.call-update) | async-done | bytes 4456464 | tf_op jit(solution)/shard_map/all_gather | solution.py:178
  142.9 10.0 %fusion.19 = bf16[2,272,256]{2,1,0:T(8,128)(2,1)S(1)} fusion(bf16[2,4352,256]{2,1,0:T(8,128)(2,1)} %all-gather.4.cloned.1.call-done, f32[2,272,4352]{2,1,0:T(8,128)} %copy-done.3, bf16[2,272,256]{2,1,0:T(8,128)(2,1)S(1)} %bitcast.220, f32[2,272]{1,0:T(2,128)S(1)} %copy.65, f32[2,272]{1,0:T(2,128)S(1)} %log_add_fusion, ...), kind=kOutput, calls=%fused_computation.44 | convolution fusion | flops 2434056192 | bytes 18944256 | tf_op jit(solution)/shard_map/shqk,skhd->sqhd/dot_general | solution.py:183
  154.2 2.6 collective-permute-done.1
  156.8 2.2 collective-permute-start.2
  159.0 3.9 collective-permute-done.2
  163.6 4.6 %collective-permute-done.3 = f32[8,2,2,272,1]{3,0,2,4,1:T(8,128)S(1)} collective-permute-done((f32[8,2,2,272,1]{3,0,2,4,1:T(8,128)S(1)}, f32[8,2,2,272,1]{3,0,2,4,1:T(8,128)S(1)}, u32[]{:S(2)}, u32[]{:S(2)}) %collective-permute-start.3) | collective-permute-done | bytes 34848 | tf_op jit(solution)/shard_map/ppermute | solution.py:43
  168.5 17.4 %all-gather.8.cloned.1.call-done = bf16[2,4352,256]{2,1,0:T(8,128)(2,1)} async-done(((bf16[2,272,256]{2,1,0:T(8,128)(2,1)}), bf16[2,4352,256]{2,1,0:T(8,128)(2,1)}) %all-gather.8.cloned.1.call-update) | async-done | bytes 4456464 | tf_op jit(solution)/shard_map/all_gather | solution.py:187
  185.9 3.8 subtract_exponential_fusion
  189.7 3.7 copy-done.2
  193.4 3.7 fusion.14
  197.1 9.0 %fusion.13 = bf16[2,272,256]{2,1,0:T(8,128)(2,1)S(1)} fusion(bf16[2,4352,256]{2,1,0:T(8,128)(2,1)} %all-gather.8.cloned.1.call-done, f32[2,4352,272]{1,2,0:T(8,128)} %copy-done.2, bf16[2,4352,256]{2,1,0:T(8,128)(2,1)} %bitcast.209, f32[2,4352]{1,0:T(2,128)S(1)} %sub.121, bf16[2,272,256]{2,0,1:T(2,128)(2,1)S(1)} %bitcast.224), kind=kOutput, calls=%fused_computation.39 | convolution fusion | flops 2431688704 | bytes 18974720 | tf_op jit(solution)/shard_map/shqk,sqhd->skhd/dot_general | solution.py:203
  206.7 2.1 collective-permute-start.8
  208.8 3.6 collective-permute-start.9
  216.9 1.7 reshape.738
  218.7 1.7 reshape.737
  230.1 1.8 multiply_reduce_fusion
  232.0 6.2 %collective-permute-start.14 = (bf16[2,1,68,256]{3,2,1,0:T(8,128)(2,1)S(1)}, bf16[2,1,68,256]{3,2,1,0:T(8,128)(2,1)S(1)}, u32[]{:S(2)}, u32[]{:S(2)}) collective-permute-start(bf16[2,1,68,256]{3,2,1,0:T(8,128)(2,1)S(1)} %get-tuple-element.41), channel_id=1, source_target_pairs={{0,1},{1,2},{2,3},{3,4},{4,5},{5,6},{6,7},{7,8},{8,9},{9,10},{10,1... | collective-permute-start | bytes 208904 | tf_op jit(solution)/shard_map/ppermute | solution.py:19
  238.2 1.9 collective-permute-start.15
  249.3 2.1 convolution_add_fusion.7
  257.0 3.0 fusion.22
  261.2 2.0 fusion.30
  270.3 3.0 copy.68
  276.7 3.9 collective-permute-start.16
  280.6 3.7 collective-permute-done.16
  284.3 2.2 select_add_fusion
  287.9 13.0 %collective-permute-done.17 = f32[221184]{0:T(1024)S(1)} collective-permute-done((f32[221184]{0:T(1024)S(1)}, f32[221184]{0:T(1024)S(1)}, u32[]{:S(2)}, u32[]{:S(2)}) %collective-permute-start.17) | collective-permute-done | bytes 884768 | tf_op jit(solution)/shard_map/ppermute | solution.py:71
  300.9 1.6 select_add_fusion.1
  302.6 8.3 %collective-permute-done.18 = f32[110592]{0:T(1024)S(1)} collective-permute-done((f32[110592]{0:T(1024)S(1)}, f32[110592]{0:T(1024)S(1)}, u32[]{:S(2)}, u32[]{:S(2)}) %collective-permute-start.18) | collective-permute-done | bytes 442400 | tf_op jit(solution)/shard_map/ppermute | solution.py:71
  311.8 5.5 %collective-permute-done.19 = f32[55296]{0:T(1024)S(1)} collective-permute-done((f32[55296]{0:T(1024)S(1)}, f32[55296]{0:T(1024)S(1)}, u32[]{:S(2)}, u32[]{:S(2)}) %collective-permute-start.19) | collective-permute-done | bytes 221216 | tf_op jit(solution)/shard_map/ppermute | solution.py:71
  317.4 6.2 %collective-permute-done.20 = f32[27648]{0:T(1024)S(1)} collective-permute-done((f32[27648]{0:T(1024)S(1)}, f32[27648]{0:T(1024)S(1)}, u32[]{:S(2)}, u32[]{:S(2)}) %collective-permute-start.20) | collective-permute-done | bytes 110624 | tf_op jit(solution)/shard_map/ppermute | solution.py:71
  323.7 2.7 collective-permute-start.21
  326.5 3.0 collective-permute-done.21
  330.3 4.4 collective-permute-done.22
  334.7 2.8 collective-permute-start.23
  337.5 4.9 %collective-permute-done.23 = f32[3456]{0:T(1024)S(1)} collective-permute-done((f32[3456]{0:T(1024)S(1)}, f32[3456]{0:T(1024)S(1)}, u32[]{:S(2)}, u32[]{:S(2)}) %collective-permute-start.23) | collective-permute-done | bytes 13856 | tf_op jit(solution)/shard_map/ppermute | solution.py:71
  342.4 2.7 collective-permute-start.24
  345.2 4.9 %collective-permute-done.24 = f32[3456]{0:T(1024)S(1)} collective-permute-done((f32[3456]{0:T(1024)S(1)}, f32[3456]{0:T(1024)S(1)}, u32[]{:S(2)}, u32[]{:S(2)}) %collective-permute-start.24) | collective-permute-done | bytes 13856 | tf_op jit(solution)/shard_map/ppermute | solution.py:74
  350.6 6.0 %collective-permute-done.25 = f32[6912]{0:T(1024)S(1)} collective-permute-done((f32[6912]{0:T(1024)S(1)}, f32[6912]{0:T(1024)S(1)}, u32[]{:S(2)}, u32[]{:S(2)}) %collective-permute-start.25) | collective-permute-done | bytes 27680 | tf_op jit(solution)/shard_map/ppermute | solution.py:74
  356.6 2.8 collective-permute-start.26
  359.4 3.6 collective-permute-done.26
  363.1 7.4 %collective-permute-done.27 = f32[27648]{0:T(1024)S(1)} collective-permute-done((f32[27648]{0:T(1024)S(1)}, f32[27648]{0:T(1024)S(1)}, u32[]{:S(2)}, u32[]{:S(2)}) %collective-permute-start.27) | collective-permute-done | bytes 110624 | tf_op jit(solution)/shard_map/ppermute | solution.py:74
  370.6 8.3 %collective-permute-done.28 = f32[55296]{0:T(1024)S(1)} collective-permute-done((f32[55296]{0:T(1024)S(1)}, f32[55296]{0:T(1024)S(1)}, u32[]{:S(2)}, u32[]{:S(2)}) %collective-permute-start.28) | collective-permute-done | bytes 221216 | tf_op jit(solution)/shard_map/ppermute | solution.py:74
  379.6 7.8 %collective-permute-done.29 = f32[110592]{0:T(1024)S(1)} collective-permute-done((f32[110592]{0:T(1024)S(1)}, f32[110592]{0:T(1024)S(1)}, u32[]{:S(2)}, u32[]{:S(2)}) %collective-permute-start.29) | collective-permute-done | bytes 442400 | tf_op jit(solution)/shard_map/ppermute | solution.py:74
  388.1 13.0 %collective-permute-done.30 = f32[221184]{0:T(1024)S(1)} collective-permute-done((f32[221184]{0:T(1024)S(1)}, f32[221184]{0:T(1024)S(1)}, u32[]{:S(2)}, u32[]{:S(2)}) %collective-permute-start.30) | collective-permute-done | bytes 884768 | tf_op jit(solution)/shard_map/ppermute | solution.py:74
  403.5 2.9 collective-permute-done.10
  406.5 3.6 collective-permute-done.11
  410.1 5.1 %collective-permute-done.12 = f32[2,2,32]{2,1,0:T(2,128)S(1)} collective-permute-done((f32[2,2,32]{2,1,0:T(2,128)S(1)}, f32[2,2,32]{2,1,0:T(2,128)S(1)}, u32[]{:S(2)}, u32[]{:S(2)}) %collective-permute-start.12) | collective-permute-done | bytes 544 | tf_op jit(solution)/shard_map/ppermute | solution.py:32
  415.4 3.6 collective-permute-done.13
  423.3 1.9 concatenate.347
  425.2 2.5 maximum_select_fusion.4
  428.9 3.5 maximum_select_fusion.2
  432.3 3.0 maximum_select_fusion
  436.2 1.8 reshape.755
  439.0 1.8 concatenate.345
  440.8 1.7 fusion.37
  (267 shorter events, 68.3 us)
Async XLA Ops:
  7.2 199.0 %copy-start = (bf16[256,768]{1,0:T(8,128)(2,1)S(1)}, bf16[256,768]{1,0:T(8,128)(2,1)}, u32[]{:S(2)}) copy-start(bf16[256,768]{1,0:T(8,128)(2,1)} %param.18) | copy-start | bytes 1179652
  7.2 4.1 copy-start.30
  7.2 5.1 %copy-start.31 = (bf16[2,4,68,256]{3,1,2,0:T(4,128)(2,1)S(1)}, bf16[2,4,68,256]{3,1,2,0:T(4,128)(2,1)}, u32[]{:S(2)}) copy-start(bf16[2,4,68,256]{3,1,2,0:T(4,128)(2,1)} %param.16) | copy-start | bytes 835588
  7.2 5.2 %copy-start.35 = (bf16[256,256]{1,0:T(8,128)(2,1)S(1)}, bf16[256,256]{1,0:T(8,128)(2,1)}, u32[]{:S(2)}) copy-start(bf16[256,256]{1,0:T(8,128)(2,1)} %param.19) | copy-start | bytes 393220
  7.2 101.8 %all-gather.4.cloned.1.call-start = ((), (), s32[]{:S(2)}) async-start(), calls=%async_computation.1 | async-start | bytes 4734976 | tf_op jit(solution)/shard_map/all_gather | solution.py:177
  9.3 133.6 %all-gather.6.cloned.1.call-start = ((), (), s32[]{:S(2)}) async-start(), calls=%async_computation.2 | async-start | bytes 4734976 | tf_op jit(solution)/shard_map/all_gather | solution.py:178
  11.2 174.7 %all-gather.8.cloned.1.call-start = ((), (), s32[]{:S(2)}) async-start(), calls=%async_computation.3 | async-start | bytes 4734976 | tf_op jit(solution)/shard_map/all_gather | solution.py:187
  15.2 5.8 %copy-start.8 = (bf16[2,4,68,256]{3,1,2,0:T(4,128)(2,1)S(1)}, bf16[2,4,68,256]{3,1,2,0:T(4,128)(2,1)}, u32[]{:S(2)}) copy-start(bf16[2,4,68,256]{3,1,2,0:T(4,128)(2,1)} %param.11) | copy-start | bytes 835588
  15.2 6.5 %copy-start.32 = (bf16[2,4,68,256]{3,1,2,0:T(4,128)(2,1)S(1)}, bf16[2,4,68,256]{3,1,2,0:T(4,128)(2,1)}, u32[]{:S(2)}) copy-start(bf16[2,4,68,256]{3,1,2,0:T(4,128)(2,1)} %param.15) | copy-start | bytes 835588
  15.2 89.1 %all-to-all-start = ((bf16[16,2,272,256]{3,2,1,0:T(8,128)(2,1)}), bf16[16,2,272,256]{3,2,1,0:T(8,128)(2,1)}, u32[]{:S(2)}, u32[]{:S(2)}) async-start(bf16[16,2,272,256]{3,2,1,0:T(8,128)(2,1)} %stack.59), calls=%async_computation | async-start | bytes 8912896 | tf_op jit(solution)/shard_map/all_to_all | solution.py:189
  21.5 2.2 collective-permute-start.4
  22.4 86.7 %copy-start.11 = (f32[32,2,8,128]{3,1,2,0:T(2,128)}, f32[32,2,8,128]{3,1,2,0:T(2,128)S(1)}, u32[]{:S(2)}) copy-start(f32[32,2,8,128]{3,1,2,0:T(2,128)S(1)} %copy.67) | copy-start | bytes 786436
  23.7 71.9 %collective-permute-start.5 = (f32[2,2,32]{2,1,0:T(2,128)S(1)}, f32[2,2,32]{2,1,0:T(2,128)S(1)}, u32[]{:S(2)}, u32[]{:S(2)}) collective-permute-start(f32[2,2,32]{2,1,0:T(2,128)S(1)} %fusion.94), channel_id=1, source_target_pairs={{0,2},{1,3},{2,0},{3,1},{4,6},{5,7},{6,4},{7,5},{8,10},{9,11},{10,... | collective-permute-start | bytes 1544 | tf_op jit(solution)/shard_map/ppermute | solution.py:32
  95.7 5.1 %collective-permute-start.6 = (f32[2,2,32]{2,1,0:T(2,128)S(1)}, f32[2,2,32]{2,1,0:T(2,128)S(1)}, u32[]{:S(2)}, u32[]{:S(2)}) collective-permute-start(f32[2,2,32]{2,1,0:T(2,128)S(1)} %fusion.154), channel_id=1, source_target_pairs={{0,4},{1,5},{2,6},{3,7},{4,0},{5,1},{6,2},{7,3},{8,12},{9,13},{10,... | collective-permute-start | bytes 1544 | tf_op jit(solution)/shard_map/ppermute | solution.py:32
  100.7 3.6 collective-permute-start.7
  112.9 3.7 copy-start.3
  116.6 36.3 %collective-permute-start = (f32[1,2,2,272,1]{3,4,2,1,0:T(1,128)S(1)}, f32[1,2,2,272,1]{3,4,2,1,0:T(1,128)S(1)}, u32[]{:S(2)}, u32[]{:S(2)}) collective-permute-start(f32[1,2,2,272,1]{3,4,2,1,0:T(1,128)S(1)} %get-tuple-element.50), channel_id=1, source_target_pairs={{0,1},{1,0},{2,3},{3,2},{4,5},{5,4},{6,7},{7,6},{8,9},{9,8},{10,11... | collective-permute-start | bytes 13064 | tf_op jit(solution)/shard_map/ppermute | solution.py:43
  152.9 53.2 %copy-start.40 = (bf16[2,272,256]{2,1,0:T(8,128)(2,1)}, bf16[2,272,256]{2,1,0:T(8,128)(2,1)S(1)}, u32[]{:S(2)}) copy-start(bf16[2,272,256]{2,1,0:T(8,128)(2,1)S(1)} %fusion.19) | copy-start | bytes 835588
  153.0 3.8 collective-permute-start.1
  156.8 6.1 %collective-permute-start.2 = (f32[4,2,2,272,1]{3,0,2,1,4:T(4,128)S(1)}, f32[4,2,2,272,1]{3,0,2,1,4:T(4,128)S(1)}, u32[]{:S(2)}, u32[]{:S(2)}) collective-permute-start(f32[4,2,2,272,1]{3,0,2,1,4:T(4,128)S(1)} %maximum_select_fusion.14), channel_id=1, source_target_pairs={{0,4},{1,5},{2,6},{3,7},{4,0},{5,1},{6,2},{7,3},{8,12},{9,13},{10,... | collective-permute-start | bytes 52232 | tf_op jit(solution)/shard_map/ppermute | solution.py:43
  162.9 5.3 %collective-permute-start.3 = (f32[8,2,2,272,1]{3,0,2,4,1:T(8,128)S(1)}, f32[8,2,2,272,1]{3,0,2,4,1:T(8,128)S(1)}, u32[]{:S(2)}, u32[]{:S(2)}) collective-permute-start(f32[8,2,2,272,1]{3,0,2,4,1:T(8,128)S(1)} %fusion.81), channel_id=1, source_target_pairs={{0,8},{1,9},{2,10},{3,11},{4,12},{5,13},{6,14},{7,15},{8,0},{9,1},... | collective-permute-start | bytes 104456 | tf_op jit(solution)/shard_map/ppermute | solution.py:43
  189.7 3.7 copy-start.2
  193.4 3.7 copy-start.19
  197.1 9.0 %copy-start.28 = (bf16[2,256,272]{1,2,0:T(8,128)(2,1)}, bf16[2,256,272]{1,2,0:T(8,128)(2,1)S(1)}, u32[]{:S(2)}) copy-start(bf16[2,256,272]{1,2,0:T(8,128)(2,1)S(1)} %fusion.14) | copy-start | bytes 835588
  206.1 2.7 copy-start.33
  206.7 6.1 %collective-permute-start.8 = (bf16[2,1,68,256]{3,2,1,0:T(8,128)(2,1)S(1)}, bf16[2,1,68,256]{3,2,1,0:T(8,128)(2,1)S(1)}, u32[]{:S(2)}, u32[]{:S(2)}) collective-permute-start(bf16[2,1,68,256]{3,2,1,0:T(8,128)(2,1)S(1)} %get-tuple-element.45), channel_id=1, source_target_pairs={{0,1},{1,2},{2,3},{3,4},{4,5},{5,6},{6,7},{7,8},{8,9},{9,10},{10,1... | collective-permute-start | bytes 208904 | tf_op jit(solution)/shard_map/ppermute | solution.py:19
  208.8 5.4 %collective-permute-start.9 = (bf16[2,1,68,256]{3,2,1,0:T(8,128)(2,1)S(1)}, bf16[2,1,68,256]{3,2,1,0:T(8,128)(2,1)S(1)}, u32[]{:S(2)}, u32[]{:S(2)}) collective-permute-start(bf16[2,1,68,256]{3,2,1,0:T(8,128)(2,1)S(1)} %get-tuple-element.46), channel_id=1, source_target_pairs={{1,0},{2,1},{3,2},{4,3},{5,4},{6,5},{7,6},{8,7},{9,8},{10,9},{11,1... | collective-permute-start | bytes 208904 | tf_op jit(solution)/shard_map/ppermute | solution.py:21
  215.9 6.1 %copy-start.10 = (bf16[9,256,256]{2,1,0:T(8,128)(2,1)S(1)}, bf16[9,256,256]{2,1,0:T(8,128)(2,1)}, u32[]{:S(2)}) copy-start(bf16[9,256,256]{2,1,0:T(8,128)(2,1)} %param.17) | copy-start | bytes 3538948
  221.2 3.5 copy-start.25
  232.0 9.1 %collective-permute-start.14 = (bf16[2,1,68,256]{3,2,1,0:T(8,128)(2,1)S(1)}, bf16[2,1,68,256]{3,2,1,0:T(8,128)(2,1)S(1)}, u32[]{:S(2)}, u32[]{:S(2)}) collective-permute-start(bf16[2,1,68,256]{3,2,1,0:T(8,128)(2,1)S(1)} %get-tuple-element.41), channel_id=1, source_target_pairs={{0,1},{1,2},{2,3},{3,4},{4,5},{5,6},{6,7},{7,8},{8,9},{9,10},{10,1... | collective-permute-start | bytes 208904 | tf_op jit(solution)/shard_map/ppermute | solution.py:19
  238.2 3.9 collective-permute-start.15
  246.0 9.1 %copy-start.15 = (bf16[544,256]{1,0:T(8,128)(2,1)}, bf16[544,256]{1,0:T(8,128)(2,1)S(1)}, u32[]{:S(2)}) copy-start(bf16[544,256]{1,0:T(8,128)(2,1)S(1)} %reshape.747) | copy-start | bytes 835588
  247.2 6.6 %copy-start.17 = (bf16[544,256]{1,0:T(8,128)(2,1)}, bf16[544,256]{1,0:T(8,128)(2,1)S(1)}, u32[]{:S(2)}) copy-start(bf16[544,256]{1,0:T(8,128)(2,1)S(1)} %reshape.746) | copy-start | bytes 835588
  252.4 3.0 copy-start.13
  260.0 3.3 copy-start.18
  260.0 4.3 copy-start.16
  261.2 7.1 %copy-start.22 = (bf16[544,256]{1,0:T(8,128)(2,1)S(1)}, bf16[544,256]{1,0:T(8,128)(2,1)}, u32[]{:S(2)}) copy-start(bf16[544,256]{1,0:T(8,128)(2,1)} %reshape.751) | copy-start | bytes 835588
  263.3 6.1 %copy-start.14 = (bf16[544,256]{1,0:T(8,128)(2,1)S(1)}, bf16[544,256]{1,0:T(8,128)(2,1)}, u32[]{:S(2)}) copy-start(bf16[544,256]{1,0:T(8,128)(2,1)} %copy-done.13) | copy-start | bytes 835588
  270.3 3.0 copy-start.5
  276.7 7.6 %collective-permute-start.16 = (f32[442368]{0:T(1024)}, f32[442368]{0:T(1024)}, u32[]{:S(2)}, u32[]{:S(2)}) collective-permute-start(f32[442368]{0:T(1024)} %fusion.6), channel_id=1, source_target_pairs={{0,1},{1,0},{2,3},{3,2},{4,5},{5,4},{6,7},{7,6},{8,9},{9,8},{10,11... | collective-permute-start | bytes 5308424 | tf_op jit(solution)/shard_map/ppermute | solution.py:71
  287.8 13.1 %collective-permute-start.17 = (f32[221184]{0:T(1024)S(1)}, f32[221184]{0:T(1024)S(1)}, u32[]{:S(2)}, u32[]{:S(2)}) collective-permute-start(f32[221184]{0:T(1024)S(1)} %slice_select_fusion), channel_id=1, source_target_pairs={{0,2},{1,17},{2,0},{3,19},{4,6},{5,21},{6,4},{7,23},{8,10},{9,25},... | collective-permute-start | bytes 2654216 | tf_op jit(solution)/shard_map/ppermute | solution.py:71
  302.5 8.4 %collective-permute-start.18 = (f32[110592]{0:T(1024)S(1)}, f32[110592]{0:T(1024)S(1)}, u32[]{:S(2)}, u32[]{:S(2)}) collective-permute-start(f32[110592]{0:T(1024)S(1)} %slice_select_fusion.1), channel_id=1, source_target_pairs={{0,8},{1,3},{2,10},{3,1},{4,12},{5,7},{6,14},{7,5},{8,0},{9,11},{1... | collective-permute-start | bytes 1327112 | tf_op jit(solution)/shard_map/ppermute | solution.py:71
  311.0 6.2 %collective-permute-start.19 = (f32[55296]{0:T(1024)S(1)}, f32[55296]{0:T(1024)S(1)}, u32[]{:S(2)}, u32[]{:S(2)}) collective-permute-start(f32[55296]{0:T(1024)S(1)} %slice_select_fusion.2), channel_id=1, source_target_pairs={{0,16},{1,9},{2,18},{3,11},{4,20},{5,13},{6,22},{7,15},{8,24},{9,1... | collective-permute-start | bytes 663560 | tf_op jit(solution)/shard_map/ppermute | solution.py:71
  317.3 6.3 %collective-permute-start.20 = (f32[27648]{0:T(1024)S(1)}, f32[27648]{0:T(1024)S(1)}, u32[]{:S(2)}, u32[]{:S(2)}) collective-permute-start(f32[27648]{0:T(1024)S(1)} %slice_select_fusion.3), channel_id=1, source_target_pairs={{0,4},{1,33},{2,6},{3,35},{4,0},{5,37},{6,2},{7,39},{8,12},{9,41},... | collective-permute-start | bytes 331784 | tf_op jit(solution)/shard_map/ppermute | solution.py:71
  323.7 5.8 %collective-permute-start.21 = (f32[13824]{0:T(1024)S(1)}, f32[13824]{0:T(1024)S(1)}, u32[]{:S(2)}, u32[]{:S(2)}) collective-permute-start(f32[13824]{0:T(1024)S(1)} %slice_select_fusion.4), channel_id=1, source_target_pairs={{0,128},{1,5},{2,130},{3,7},{4,132},{5,1},{6,134},{7,3},{8,136},{9... | collective-permute-start | bytes 165896 | tf_op jit(solution)/shard_map/ppermute | solution.py:71
  329.5 5.2 %collective-permute-start.22 = (f32[6912]{0:T(1024)S(1)}, f32[6912]{0:T(1024)S(1)}, u32[]{:S(2)}, u32[]{:S(2)}) collective-permute-start(f32[6912]{0:T(1024)S(1)} %slice_select_fusion.5), channel_id=1, source_target_pairs={{0,32},{1,129},{2,34},{3,131},{4,36},{5,133},{6,38},{7,135},{8,40}... | collective-permute-start | bytes 82952 | tf_op jit(solution)/shard_map/ppermute | solution.py:71
  334.7 7.7 %collective-permute-start.23 = (f32[3456]{0:T(1024)S(1)}, f32[3456]{0:T(1024)S(1)}, u32[]{:S(2)}, u32[]{:S(2)}) collective-permute-start(f32[3456]{0:T(1024)S(1)} %slice_select_fusion.6), channel_id=1, source_target_pairs={{0,64},{1,65},{2,66},{3,67},{4,68},{5,69},{6,70},{7,71},{8,72},{9,... | collective-permute-start | bytes 41480 | tf_op jit(solution)/shard_map/ppermute | solution.py:71
  342.4 7.6 %collective-permute-start.24 = (f32[3456]{0:T(1024)S(1)}, f32[3456]{0:T(1024)S(1)}, u32[]{:S(2)}, u32[]{:S(2)}) collective-permute-start(f32[3456]{0:T(1024)S(1)} %select_add_fusion.7), channel_id=1, source_target_pairs={{0,64},{1,65},{2,66},{3,67},{4,68},{5,69},{6,70},{7,71},{8,72},{9,... | collective-permute-start | bytes 41480 | tf_op jit(solution)/shard_map/ppermute | solution.py:74
  350.1 6.5 %collective-permute-start.25 = (f32[6912]{0:T(1024)S(1)}, f32[6912]{0:T(1024)S(1)}, u32[]{:S(2)}, u32[]{:S(2)}) collective-permute-start(f32[6912]{0:T(1024)S(1)} %maximum_select_fusion.13), channel_id=1, source_target_pairs={{0,32},{1,129},{2,34},{3,131},{4,36},{5,133},{6,38},{7,135},{8,40}... | collective-permute-start | bytes 82952 | tf_op jit(solution)/shard_map/ppermute | solution.py:74
  356.6 6.4 %collective-permute-start.26 = (f32[13824]{0:T(1024)S(1)}, f32[13824]{0:T(1024)S(1)}, u32[]{:S(2)}, u32[]{:S(2)}) collective-permute-start(f32[13824]{0:T(1024)S(1)} %maximum_select_fusion.10), channel_id=1, source_target_pairs={{0,128},{1,5},{2,130},{3,7},{4,132},{5,1},{6,134},{7,3},{8,136},{9... | collective-permute-start | bytes 165896 | tf_op jit(solution)/shard_map/ppermute | solution.py:74
  363.0 7.5 %collective-permute-start.27 = (f32[27648]{0:T(1024)S(1)}, f32[27648]{0:T(1024)S(1)}, u32[]{:S(2)}, u32[]{:S(2)}) collective-permute-start(f32[27648]{0:T(1024)S(1)} %maximum_select_fusion.8), channel_id=1, source_target_pairs={{0,4},{1,33},{2,6},{3,35},{4,0},{5,37},{6,2},{7,39},{8,12},{9,41},... | collective-permute-start | bytes 331784 | tf_op jit(solution)/shard_map/ppermute | solution.py:74
  370.5 8.4 %collective-permute-start.28 = (f32[55296]{0:T(1024)S(1)}, f32[55296]{0:T(1024)S(1)}, u32[]{:S(2)}, u32[]{:S(2)}) collective-permute-start(f32[55296]{0:T(1024)S(1)} %maximum_select_fusion.7), channel_id=1, source_target_pairs={{0,16},{1,9},{2,18},{3,11},{4,20},{5,13},{6,22},{7,15},{8,24},{9,1... | collective-permute-start | bytes 663560 | tf_op jit(solution)/shard_map/ppermute | solution.py:74
  378.9 23.8 %copy-start.36 = (f32[2,256]{1,0:T(2,128)S(1)}, f32[2,256]{1,0:T(2,128)}, u32[]{:S(2)}) copy-start(f32[2,256]{1,0:T(2,128)} %get-tuple-element.20) | copy-start | bytes 6148
  379.0 8.4 %collective-permute-start.29 = (f32[110592]{0:T(1024)S(1)}, f32[110592]{0:T(1024)S(1)}, u32[]{:S(2)}, u32[]{:S(2)}) collective-permute-start(f32[110592]{0:T(1024)S(1)} %maximum_select_fusion.5), channel_id=1, source_target_pairs={{0,8},{1,3},{2,10},{3,1},{4,12},{5,7},{6,14},{7,5},{8,0},{9,11},{1... | collective-permute-start | bytes 1327112 | tf_op jit(solution)/shard_map/ppermute | solution.py:74
  388.1 31.2 %copy-start.9 = (bf16[2,4,68,256]{3,1,2,0:T(4,128)(2,1)S(1)}, bf16[2,4,68,256]{3,1,2,0:T(4,128)(2,1)}, u32[]{:S(2)}) copy-start(bf16[2,4,68,256]{3,1,2,0:T(4,128)(2,1)} %param.11) | copy-start | bytes 835588
  388.1 31.2 %copy-start.38 = (f32[256]{0:T(256)S(1)}, f32[256]{0:T(256)}, u32[]{:S(2)}) copy-start(f32[256]{0:T(256)} %param.20) | copy-start | bytes 3076
  388.1 13.0 %collective-permute-start.30 = (f32[221184]{0:T(1024)S(1)}, f32[221184]{0:T(1024)S(1)}, u32[]{:S(2)}, u32[]{:S(2)}) collective-permute-start(f32[221184]{0:T(1024)S(1)} %maximum_select_fusion.3), channel_id=1, source_target_pairs={{0,2},{1,17},{2,0},{3,19},{4,6},{5,21},{6,4},{7,23},{8,10},{9,25},... | collective-permute-start | bytes 2654216 | tf_op jit(solution)/shard_map/ppermute | solution.py:74
  402.6 29.8 %collective-permute-start.31 = (f32[442368]{0:T(1024)}, f32[442368]{0:T(1024)S(1)}, u32[]{:S(2)}, u32[]{:S(2)}) collective-permute-start(f32[442368]{0:T(1024)} %maximum_select_fusion.1), channel_id=1, source_target_pairs={{0,1},{1,0},{2,3},{3,2},{4,5},{5,4},{6,7},{7,6},{8,9},{9,8},{10,11... | collective-permute-start | bytes 5308424 | tf_op jit(solution)/shard_map/ppermute | solution.py:74
  403.0 3.5 collective-permute-start.10
  406.5 3.6 collective-permute-start.11
  410.1 5.1 %collective-permute-start.12 = (f32[2,2,32]{2,1,0:T(2,128)S(1)}, f32[2,2,32]{2,1,0:T(2,128)S(1)}, u32[]{:S(2)}, u32[]{:S(2)}) collective-permute-start(f32[2,2,32]{2,1,0:T(2,128)S(1)} %fusion.153), channel_id=1, source_target_pairs={{0,4},{1,5},{2,6},{3,7},{4,0},{5,1},{6,2},{7,3},{8,12},{9,13},{10,... | collective-permute-start | bytes 1544 | tf_op jit(solution)/shard_map/ppermute | solution.py:32
  415.2 3.8 collective-permute-start.13
  432.3 3.0 copy-start.7
  438.9 3.5 copy-start.1
  (13 other events, 22.4 us)
Sparse Core Ops, SparseCore 0:
  10.4 88.3 all-gather.3
  101.2 41.6 all-gather.5
  145.3 40.6 all-gather.7
